TPU v7x, 256 devices: a whole 4x4x8 slice. The times are simulated.
256 devices in a mesh: seq: 32 (over z, x), tp: 8 (over y, core).
Axes of the slice: x: 4, y: 4, z: 8, core: 2. Of those that a mesh axis runs over, the one named last changes fastest.
Arguments:
- prefill_states: bfloat16 [8192, 1536], P('seq'), may hold values from -6 to 6
- decode_states: bfloat16 [256, 1536], P(('seq', 'tp')), may hold values from -6 to 6
- attn_gain: bfloat16 [1536], replicated, may hold values from 0.25 to 1.75
- query_weight: bfloat16 [1536, 1536], P(None, 'tp'), may hold values from -0.625 to 0.625
- keyvalue_weight: bfloat16 [1536, 8, 128], P(None, 'tp'), as said below
- output_weight: bfloat16 [1536, 1536], P('tp'), may hold values from -0.3125 to 0.3125
- cache_keyval: bfloat16 [256, 2048, 8, 128], P(None, 'seq', 'tp'), may hold values from -68 to 68, as said below
- cached_length: int32 [256], replicated, may hold values from 1 to 2048, as said below
- span_tenant: int32 [4], replicated, may hold values from 0 to 3
- ffn_gain: bfloat16 [1536], replicated, may hold values from 0.25 to 1.75
- expert_in: bfloat16 [32, 1536, 1024], P('seq'), may hold values from -0.15625 to 0.15625
- expert_out: bfloat16 [32, 512, 1536], P('seq'), may hold values from -0.25 to 0.25
- routes: int32 [8448, 8], P(('seq', 'tp')), may hold values from 0 to 31, all different within a row; in each aligned block of 33 rows (0 to 32, 33 to 65, ...) at most 18 rows name the same one
- gate_values: float32 [8448, 8], P(('seq', 'tp')), may hold values from 0.05 to 0.3
Outputs:
- prefill_out: bfloat16 [8192, 1536], P(('seq', 'tp'))
- decode_out: bfloat16 [256, 1536], P(('seq', 'tp'))
Inputs may be any that keep to these rules, and one draw needn't show every extreme that they name: `cached_length`: positions at or beyond a request's length hold no key; the new token stands at that length. `cache_keyval`: keys are rotated at their positions. `keyvalue_weight`: keys first, then values, in each head. `routes`: in the rows of one device no expert is named more than 18 times, a bound that some block reaches.
All inputs are finite; a program needn't handle non-finite values.
Results may differ from a plain program's by a relative error of at most 0.02.
The roundings to bfloat16 on the way count: a program that leaves them out, or rounds other values in their place, can miss the bound.
Values may be sent and summed in bfloat16 or wider, within the bound.
No kernel may reach another device: no remote copies, remote signals or barrier semaphores. Data moves between devices by JAX's collectives and lax.ppermute only.
A program may use at most 128 MiB of HBM per device.

v0:
```python
import math

import jax
import jax.numpy as jnp
from jax import lax
from jax.sharding import PartitionSpec as P
from jax.experimental import pallas as pl
from jax.experimental.pallas import tpu as pltpu

EXPERTS = 32
SPAN = 2048


eps_norm = 1e-05
rope_base = 10000.0
masked_score = -1e30
key_block = 512


def rms_norm(values, scales):
    floats = values.astype(jnp.float32)
    factor = lax.rsqrt(jnp.mean(floats * floats, axis=-1, keepdims=True) + eps_norm)
    return (floats * factor * scales.astype(jnp.float32)).astype(jnp.bfloat16)


def apply_rotary(values, token_positions):
    half_dim = values.shape[-1] // 2
    frequency = rope_base ** (-2.0 * jnp.arange(half_dim, dtype=jnp.float32) / values.shape[-1])
    angles = token_positions.astype(jnp.float32)[:, None] * frequency[None, :]
    cosine = jnp.cos(angles)[:, None, :]
    sine_part = jnp.sin(angles)[:, None, :]
    first_half = values[..., :half_dim]
    second_half = values[..., half_dim:]
    return jnp.concatenate(
        [
            first_half * cosine - second_half * sine_part,
            second_half * cosine + first_half * sine_part,
        ],
        axis=-1,
    )


def span_tables(span_tenant):
    span_count = span_tenant.shape[0]
    ordinal = jnp.arange(span_count, dtype=jnp.int32)
    same_tenant = span_tenant[:, None] == span_tenant[None, :]
    earlier = ordinal[None, :] < ordinal[:, None]
    return jnp.sum(jnp.where(same_tenant & earlier, 1, 0), axis=1).astype(jnp.int32)


def token_tables(token_index, span_tenant, before):
    span_count = span_tenant.shape[0]
    span_index = token_index // SPAN
    onehot = span_index[:, None] == jnp.arange(span_count, dtype=jnp.int32)[None, :]
    tenant = jnp.sum(jnp.where(onehot, span_tenant[None, :], 0), axis=1)
    offset = jnp.sum(jnp.where(onehot, before[None, :], 0), axis=1)
    return (tenant, offset * SPAN + token_index % SPAN)


def attend_keys(fold_state, keyvalue_rows, visible, query_matrix, score_scale):
    run_max, run_total, run_acc = fold_state
    head_dim = keyvalue_rows.shape[-1] // 2
    scores = (
        jnp.einsum(
            "qhgd,khd->qhgk",
            query_matrix,
            keyvalue_rows[..., :head_dim],
            preferred_element_type=jnp.float32,
        )
        * score_scale
    )
    mask_full = visible[:, None, None, :]
    scores = jnp.where(mask_full, scores, masked_score)
    new_max = jnp.maximum(run_max, jnp.max(scores, axis=-1))
    weights_exp = jnp.where(mask_full, jnp.exp(scores - new_max[..., None]), 0.0)
    factor = jnp.exp(run_max - new_max)
    new_total = run_total * factor + jnp.sum(weights_exp, axis=-1)
    new_acc = run_acc * factor[..., None] + jnp.einsum(
        "qhgk,khd->qhgd",
        weights_exp.astype(jnp.bfloat16),
        keyvalue_rows[..., head_dim:],
        preferred_element_type=jnp.float32,
    )
    return (new_max, new_total, new_acc)


def flash_kernel(
    flags_ref, q_ref, k_ref, v_ref, row_token_ref, row_tenant_ref, key_tenant_ref,
    o_ref, max_ref, total_ref, acc_ref, *, score_scale, block_len
):
    step = pl.program_id(0)

    @pl.when(step == 0)
    def _():
        max_ref[...] = jnp.full(max_ref.shape, masked_score, jnp.float32)
        total_ref[...] = jnp.zeros(total_ref.shape, jnp.float32)
        acc_ref[...] = jnp.zeros(acc_ref.shape, jnp.float32)

    @pl.when(flags_ref[step] != 0)
    def _():
        scores = (
            lax.dot_general(
                q_ref[...], v_ref[...], (((1,), (1,)), ((), ())),
                preferred_element_type=jnp.float32,
            )
            * score_scale
        )
        key_index = step * block_len + lax.broadcasted_iota(jnp.int32, (1, block_len), 1)
        visible = (row_tenant_ref[...] == key_tenant_ref[...]) & (
            row_token_ref[...] >= key_index
        )
        scores = jnp.where(visible, scores, masked_score)
        run_max = max_ref[...]
        new_max = jnp.maximum(run_max, jnp.max(scores, axis=-1, keepdims=True))
        weights_exp = jnp.where(visible, jnp.exp(scores - new_max), 0.0)
        factor = jnp.exp(run_max - new_max)
        total_ref[...] = total_ref[...] * factor + jnp.sum(weights_exp, axis=-1, keepdims=True)
        acc_ref[...] = acc_ref[...] * factor + jnp.dot(
            weights_exp.astype(jnp.bfloat16), v_ref[...], preferred_element_type=jnp.float32
        )
        max_ref[...] = new_max

    @pl.when(step == pl.num_programs(0) - 1)
    def _():
        o_ref[...] = (acc_ref[...] / total_ref[...]).astype(o_ref.dtype)


def flash_attend(flags, queries, keyvals, head, row_token, row_tenant, key_tenant, score_scale, block_len, interpret=False):
    query_count, head_dim = queries.shape
    key_count = keyvals.shape[0]
    full = lambda step, flags_ref: (0, 0)
    grid_spec = pltpu.PrefetchScalarGridSpec(
        num_scalar_prefetch=1,
        grid=(key_count // block_len,),
        in_specs=[
            pl.BlockSpec((query_count, head_dim), full),
            pl.BlockSpec((block_len, head_dim), lambda step, flags_ref: (step, head)),
            pl.BlockSpec((block_len, head_dim), lambda step, flags_ref: (step, head)),
            pl.BlockSpec((query_count, 1), full),
            pl.BlockSpec((query_count, 1), full),
            pl.BlockSpec((1, block_len), lambda step, flags_ref: (0, step)),
        ],
        out_specs=pl.BlockSpec((query_count, head_dim), full),
        scratch_shapes=[
            pltpu.VMEM((query_count, 1), jnp.float32),
            pltpu.VMEM((query_count, 1), jnp.float32),
            pltpu.VMEM((query_count, head_dim), jnp.float32),
        ],
    )
    body = lambda *refs: flash_kernel(*refs, score_scale=score_scale, block_len=block_len)
    return pl.pallas_call(
        body,
        grid_spec=grid_spec,
        out_shape=jax.ShapeDtypeStruct((query_count, head_dim), jnp.bfloat16),
        interpret=interpret,
    )(flags, queries, keyvals, keyvals, row_token[:, None], row_tenant[:, None], key_tenant[None, :])


def swap_partner(values, axis_name, distance):
    count = lax.axis_size(axis_name)
    pairs = [(i, i ^ distance) for i in range(count)]
    return lax.ppermute(values, axis_name, pairs)


def lane_dense(values):
    flat = values.reshape(-1)
    return flat.reshape(-1, 128) if flat.shape[0] % 128 == 0 else flat.reshape(1, -1)


def gather_blocks(block, axis_name, distances):
    index = lax.axis_index(axis_name)
    shape = block.shape
    block = lane_dense(block)[None]
    stacked = block
    done = []
    for distance in distances:
        theirs = swap_partner(stacked, axis_name, distance)
        upper = (index // distance) % 2 == 1
        low = jnp.where(upper, theirs, stacked)
        high = jnp.where(upper, stacked, theirs)
        place = sum(1 for d in done if d > distance)
        stacked = jnp.stack([low, high], axis=place)
        done.append(distance)
    return stacked.reshape((-1,) + shape[1:])


def scatter_blocks(values, axis_name, distances, combine, send_type=None, dense=False):
    count = lax.axis_size(axis_name)
    index = lax.axis_index(axis_name)
    levels = count.bit_length() - 1
    rows = values.shape[0] // count
    part_shape = (rows,) + values.shape[1:]
    if dense:
        flat = math.prod(part_shape)
        part_shape = (flat // 128, 128) if flat % 128 == 0 else (1, flat)
    stacked = values.reshape((2,) * levels + part_shape)
    remaining = [count >> (j + 1) for j in range(levels)]
    for distance in distances:
        place = remaining.index(distance)
        low = lax.index_in_dim(stacked, 0, place, keepdims=False)
        high = lax.index_in_dim(stacked, 1, place, keepdims=False)
        upper = (index // distance) % 2 == 1
        keep = jnp.where(upper, high, low)
        send = jnp.where(upper, low, high)
        if send_type is not None:
            send = send.astype(send_type)
        received = swap_partner(send, axis_name, distance).astype(keep.dtype)
        stacked = combine(keep, received)
        remaining.pop(place)
    return stacked.reshape((rows,) + values.shape[1:])


def add_parts(first, second):
    return first + second


def merge_softmax(first, second, groups, head_dim):
    width = groups * head_dim
    first_max, second_max = first[..., width + groups:], second[..., width + groups:]
    top = jnp.maximum(first_max, second_max)
    first_scale = jnp.exp(first_max - top)
    second_scale = jnp.exp(second_max - top)
    acc = first[..., :width] * jnp.repeat(first_scale, head_dim, axis=-1) + second[
        ..., :width
    ] * jnp.repeat(second_scale, head_dim, axis=-1)
    total = first[..., width:width + groups] * first_scale + second[..., width:width + groups] * second_scale
    return jnp.concatenate([acc, total, top], axis=-1)

def shards(
    prefill_states,
    decode_states,
    attn_gain,
    query_weight,
    keyvalue_weight,
    output_weight,
    cache_keyval,
    cached_length,
    span_tenant,
    ffn_gain,
    expert_in,
    expert_out,
    routes,
    gate_values,
):
    seq_count = lax.axis_size("seq")
    tp_count = lax.axis_size("tp")
    seq_index = lax.axis_index("seq")
    tp_index = lax.axis_index("tp")
    pre_local, model_width = prefill_states.shape
    dec_local = decode_states.shape[0]
    heads_kv = keyvalue_weight.shape[1]
    head_dim = keyvalue_weight.shape[2] // 2
    heads_q = query_weight.shape[1] // head_dim
    query_group_count = heads_q // heads_kv
    score_scale = head_dim ** (-0.5)
    pre_share = pre_local // tp_count
    normalised_input = rms_norm(prefill_states, attn_gain)
    query_matrix = jnp.dot(
        normalised_input, query_weight, preferred_element_type=jnp.float32
    ).reshape(pre_local, heads_q, head_dim)
    keyvalue_rows = jnp.dot(
        normalised_input,
        keyvalue_weight.reshape(model_width, heads_kv * 2 * head_dim),
        preferred_element_type=jnp.float32,
    ).reshape(pre_local, heads_kv, 2 * head_dim)
    before = span_tables(span_tenant)
    token_index = seq_index * pre_local + jnp.arange(pre_local, dtype=jnp.int32)
    tenant, token_positions = token_tables(token_index, span_tenant, before)
    query_matrix = (
        apply_rotary(query_matrix, token_positions)
        .astype(jnp.bfloat16)
        .reshape(pre_local, heads_kv, query_group_count, head_dim)
    )
    rotated_keys = apply_rotary(keyvalue_rows[..., :head_dim], token_positions).astype(jnp.bfloat16)
    local_keyvals = jnp.concatenate(
        [rotated_keys, keyvalue_rows[..., head_dim:].astype(jnp.bfloat16)], axis=-1
    )
    seq_near_first = [1 << j for j in range(seq_count.bit_length() - 1)]
    key_piece = lax.all_gather(
        local_keyvals.reshape(pre_local, heads_kv * 2 * head_dim), "seq", axis=0, tiled=True
    ).reshape(-1, heads_kv, 2 * head_dim)
    piece_rows = key_piece.shape[0]
    block_len = math.gcd(piece_rows, key_block)
    blocks = key_piece.reshape(piece_rows // block_len, block_len, heads_kv, 2 * head_dim)
    query_count = pre_local * query_group_count
    query_rows = query_matrix.transpose(1, 0, 2, 3).reshape(heads_kv, query_count, head_dim)
    row_token = jnp.repeat(token_index, query_group_count)
    row_tenant = jnp.repeat(tenant, query_group_count)
    key_positions = jnp.arange(piece_rows, dtype=jnp.int32)
    key_tenant = token_tables(key_positions, span_tenant, before)[0]
    token_visible = (tenant[:, None] == key_tenant[None, :]) & (
        token_index[:, None] >= key_positions[None, :]
    )
    block_flags = jnp.any(
        token_visible.reshape(pre_local, piece_rows // block_len, block_len), axis=(0, 2)
    ).astype(jnp.int32)
    padded_queries = jnp.pad(query_rows, ((0, 0), (0, 0), (0, head_dim)))
    flat_keyvals = key_piece.reshape(piece_rows, heads_kv * 2 * head_dim)
    head_outputs = [
        flash_attend(
            block_flags,
            padded_queries[head],
            flat_keyvals,
            head,
            row_token,
            row_tenant,
            key_tenant,
            score_scale,
            block_len,
        )[:, head_dim:]
        for head in range(heads_kv)
    ]
    attended = (
        jnp.stack(head_outputs)
        .reshape(heads_kv, pre_local, query_group_count, head_dim)
        .transpose(1, 0, 2, 3)
        .reshape(pre_local, heads_q * head_dim)
    )
    prefill_part = jnp.dot(attended, output_weight, preferred_element_type=jnp.float32)
    tp_near_first = [1 << j for j in range(tp_count.bit_length() - 1)]
    prefill_sum = scatter_blocks(
        prefill_part, "tp", tp_near_first, add_parts, send_type=jnp.bfloat16, dense=True
    )
    group_states = gather_blocks(decode_states, "tp", tp_near_first[::-1])
    group_rows = group_states.shape[0]
    group_lengths = lax.dynamic_slice_in_dim(cached_length, seq_index * group_rows, group_rows, 0)
    decode_normalised = rms_norm(group_states, attn_gain)
    group_queries = jnp.dot(
        decode_normalised, query_weight, preferred_element_type=jnp.float32
    ).reshape(group_rows, heads_q, head_dim)
    group_queries = (
        apply_rotary(group_queries, group_lengths)
        .astype(jnp.bfloat16)
        .reshape(group_rows, heads_kv, query_group_count, head_dim)
    )
    decode_keyvalues = jnp.dot(
        decode_normalised,
        keyvalue_weight.reshape(model_width, heads_kv * 2 * head_dim),
        preferred_element_type=jnp.float32,
    ).reshape(group_rows, heads_kv, 2 * head_dim)
    new_keys = apply_rotary(decode_keyvalues[..., :head_dim], group_lengths).astype(jnp.bfloat16)
    new_vals = decode_keyvalues[..., head_dim:].astype(jnp.bfloat16)
    decode_queries = gather_blocks(group_queries, "seq", seq_near_first[::-1])
    cache_local = cache_keyval.shape[1]
    cache_pos = seq_index * cache_local + jnp.arange(cache_local, dtype=jnp.int32)
    visible = (cache_pos[None, :] < cached_length[:, None])[:, None, None, :]
    padded_decode = jnp.pad(decode_queries, ((0, 0), (0, 0), (0, 0), (0, head_dim)))
    scores = (
        jnp.einsum(
            "bhgd,bkhd->bhgk",
            padded_decode,
            cache_keyval,
            preferred_element_type=jnp.float32,
        )
        * score_scale
    )
    scores = jnp.where(visible, scores, masked_score)
    local_max = jnp.max(scores, axis=-1)
    weights_exp = jnp.where(visible, jnp.exp(scores - local_max[..., None]), 0.0)
    local_total = jnp.sum(weights_exp, axis=-1)
    local_acc = jnp.einsum(
        "bhgk,bkhd->bhgd",
        weights_exp.astype(jnp.bfloat16),
        cache_keyval,
        preferred_element_type=jnp.float32,
    )[..., head_dim:]
    dec_total = local_acc.shape[0]
    groups = heads_kv * query_group_count
    packed = jnp.concatenate(
        [
            local_acc.reshape(dec_total, groups * head_dim),
            local_total.reshape(dec_total, groups),
            local_max.reshape(dec_total, groups),
        ],
        axis=-1,
    )
    merged = scatter_blocks(
        packed, "seq", seq_near_first, lambda a, b: merge_softmax(a, b, groups, head_dim)
    )
    merged_acc = merged[:, : groups * head_dim].reshape(group_rows, heads_kv, query_group_count, head_dim)
    merged_total = merged[:, groups * head_dim : groups * (head_dim + 1)].reshape(
        group_rows, heads_kv, query_group_count
    )
    merged_max = merged[:, groups * (head_dim + 1) :].reshape(group_rows, heads_kv, query_group_count)
    own_score = (
        jnp.sum(
            group_queries.astype(jnp.float32) * new_keys.astype(jnp.float32)[:, :, None, :],
            axis=-1,
        )
        * score_scale
    )
    final_max = jnp.maximum(merged_max, own_score)
    rescale = jnp.exp(merged_max - final_max)
    own_exp = jnp.exp(own_score - final_max)
    final_total = merged_total * rescale + own_exp
    own_rounded = lax.optimization_barrier(own_exp.astype(jnp.bfloat16)).astype(jnp.float32)
    final_acc = (
        merged_acc * rescale[..., None]
        + own_rounded[..., None] * new_vals.astype(jnp.float32)[:, :, None, :]
    )
    decode_attended = (
        (final_acc / final_total[..., None])
        .astype(jnp.bfloat16)
        .reshape(group_rows, heads_q * head_dim)
    )
    decode_part = jnp.dot(decode_attended, output_weight, preferred_element_type=jnp.float32)
    decode_sum = scatter_blocks(decode_part, "tp", tp_near_first, add_parts, dense=True)
    own_states = lax.dynamic_slice_in_dim(prefill_states, tp_index * pre_share, pre_share, 0)
    prefill_h = (own_states.astype(jnp.float32) + prefill_sum).astype(jnp.bfloat16)
    decode_h = (decode_states.astype(jnp.float32) + decode_sum).astype(jnp.bfloat16)
    moe_in = jnp.concatenate([prefill_h, decode_h], axis=0)
    normed_moe = rms_norm(moe_in, ffn_gain)
    rows_dev, top_count = routes.shape
    capacity = 2 * ((rows_dev * top_count + EXPERTS - 1) // EXPERTS)
    capacity = -(-capacity // 8) * 8
    flat_routes = routes.reshape(rows_dev * top_count)
    expert_ids = jnp.arange(EXPERTS, dtype=jnp.int32)
    onehot = (flat_routes[:, None] == expert_ids[None, :]).astype(jnp.int32)
    slot_rank = jnp.sum(jnp.cumsum(onehot, axis=0) * onehot, axis=1) - 1
    slot_index = flat_routes * capacity + slot_rank
    repeated = jnp.repeat(normed_moe, top_count, axis=0)
    buffer = jnp.zeros((EXPERTS * capacity, model_width), jnp.bfloat16).at[slot_index].set(repeated)
    outgoing = buffer.reshape(seq_count, EXPERTS // seq_count, capacity, model_width)
    hidden = jnp.einsum(
        "secd,edf->secf",
        lax.all_to_all(outgoing, "seq", split_axis=0, concat_axis=0, tiled=True),
        expert_in,
        preferred_element_type=jnp.float32,
    )
    ff_width = expert_out.shape[1]
    active = (jax.nn.silu(hidden[..., :ff_width]) * hidden[..., ff_width:]).astype(jnp.bfloat16)
    results = jnp.einsum(
        "secf,efd->secd", active, expert_out, preferred_element_type=jnp.float32
    ).astype(jnp.bfloat16)
    returned = lax.all_to_all(results, "seq", split_axis=0, concat_axis=0, tiled=True)
    fetched = (
        returned.reshape(EXPERTS * capacity, model_width)[slot_index]
        .astype(jnp.float32)
        .reshape(rows_dev, top_count, model_width)
    )
    combined = jnp.sum(fetched * gate_values[..., None], axis=1)
    layer_out = (moe_in.astype(jnp.float32) + combined).astype(jnp.bfloat16)
    return (layer_out[:pre_share], layer_out[pre_share:])


def solution(mesh):
    return jax.shard_map(
        shards,
        mesh=mesh,
        in_specs=(
            P("seq", None),
            P(("seq", "tp"), None),
            P(),
            P(None, "tp"),
            P(None, "tp", None),
            P("tp", None),
            P(None, "seq", "tp", None),
            P(),
            P(),
            P(),
            P("seq", None, None),
            P("seq", None, None),
            P(("seq", "tp"), None),
            P(("seq", "tp"), None),
        ),
        out_specs=(P(("seq", "tp"), None), P(("seq", "tp"), None)),
        check_vma=False,
    )
```

profile of v0, /device:TPU:10, one launch (start us, length us, event | category | flops | bytes accessed | tf_op | source)
XLA Modules:
  0.0 323.2 jit_solution(13687451116556802642)
XLA Ops:
  11.7 1.7 convolution_bitcast_fusion
  14.8 2.4 collective-permute-start.3
  19.0 1.8 fusion.58
  26.3 2.2 subtract_convert_fusion
  28.5 2.9 and_reduce_fusion
  32.9 1.4 collective-permute-start.4
  35.1 1.6 collective-permute-done.4
  40.0 7.2 %collective-permute-start.6 = (bf16[1,12,128]{2,1,0:T(8,128)(2,1)S(1)}, bf16[1,12,128]{2,1,0:T(8,128)(2,1)S(1)}, u32[]{:S(2)}, u32[]{:S(2)}) collective-permute-start(bf16[1,12,128]{2,1,0:T(8,128)(2,1)S(1)} %convert_element_type.254), channel_id=1, source_target_pairs={{0,128},{8,136},{16,144},{24,152},{32,160},{40,168},{48,176},{56,1... | collective-permute-start | bytes 9224 | tf_op jit(solution)/shard_map/ppermute | solution.py:162
  47.2 1.4 broadcast_compare_fusion
  48.8 2.1 collective-permute-start.7
  51.6 1.8 collective-permute-done.7
  55.4 1.9 collective-permute-done.8
  57.3 2.2 collective-permute-start.9
  60.2 1.8 concatenate.95
  62.9 1.6 collective-permute-start.10
  64.5 1.8 fusion.62.refs_1_
  66.4 2.3 dot_general.58
  69.7 4.7 %fusion.131 = (f32[256,3]{1,0:T(8,128)S(1)}, f32[256,3,64]{2,1,0:T(4,128)S(1)}) fusion(bf16[256,64,1,128]{3,1,2,0:T(8,128)(2,1)} %param.20, bf16[256,1,3,64]{3,2,0,1:T(4,128)(2,1)S(1)} %reshape.904, pred[256,64]{1,0:T(8,128)(4,1)} %broadcast_compare_fusion), kind=kOutput, calls=%fused_computation.296 | convolution fusion | flops 12729600 | bytes 4508672 | tf_op jit(solution)/shard_map/bhgd,bkhd->bhgk/dot_general | solution.py:349
  75.7 1.4 fusion.45
  78.2 1.4 concatenate.100
  81.4 1.8 fusion.132
  83.2 2.6 collective-permute-done.11
  91.6 1.6 collective-permute-start.12
  93.2 1.5 fusion.119
  94.6 2.8 collective-permute-done.12
  101.4 2.2 collective-permute-done.13
  104.2 2.1 collective-permute-start.14
  107.0 1.9 collective-permute-done.14
  109.5 6.0 %collective-permute-start.15 = (f32[8,198]{1,0:T(8,128)S(1)}, f32[8,198]{1,0:T(8,128)S(1)}, u32[]{:S(2)}, u32[]{:S(2)}) collective-permute-start(f32[8,198]{1,0:T(8,128)S(1)} %get-tuple-element.46), channel_id=1, source_target_pairs={{0,128},{8,136},{16,144},{24,152},{32,160},{40,168},{48,176},{56,1... | collective-permute-start | bytes 19016 | tf_op jit(solution)/shard_map/ppermute | solution.py:162
  115.7 1.4 collective-permute-done.15
  125.0 1.6 collective-permute-start.17
  126.6 11.6 %shard_map.149 = bf16[768,128]{1,0:T(8,128)(2,1)} custom-call(s32[16]{0:T(128)} %convert_element_type.234.refs_0_, bf16[768,128]{1,0:T(8,128)(2,1)} %fusion.62.refs_1_, bf16[8192,128]{1,0:T(8,128)(2,1)} %bitcast.338, bf16[8192,128]{1,0:T(8,128)(2,1)} %bitcast.339, s32[768,1]{1,0:T(8,128)} %broadcast_in_dim_reshape.9.refs_4_, ...), custom_call_target="tpu_custom_call" | custom-call | tf_op jit(solution)/shard_map/pallas_call | solution.py:151
  139.5 2.6 fusion.133
  142.1 2.5 reshape.902
  144.5 1.4 fusion.38
  147.8 1.5 fusion.32
  149.3 1.5 collective-permute-start.1
  151.5 4.9 %collective-permute-done.1 = bf16[2,384,128]{2,1,0:T(8,128)(2,1)S(1)} collective-permute-done((bf16[2,384,128]{2,1,0:T(8,128)(2,1)S(1)}, bf16[2,384,128]{2,1,0:T(8,128)(2,1)S(1)}, u32[]{:S(2)}, u32[]{:S(2)}) %collective-permute-start.1) | collective-permute-done | bytes 196640 | tf_op jit(solution)/shard_map/ppermute | solution.py:162
  156.5 2.0 collective-permute-start.2
  158.5 4.2 %collective-permute-done.2 = bf16[384,128]{1,0:T(8,128)(2,1)S(1)} collective-permute-done((bf16[384,128]{1,0:T(8,128)(2,1)S(1)}, bf16[384,128]{1,0:T(8,128)(2,1)S(1)}, u32[]{:S(2)}, u32[]{:S(2)}) %collective-permute-start.2) | collective-permute-done | bytes 98336 | tf_op jit(solution)/shard_map/ppermute | solution.py:162
  165.6 3.6 %scatter_custom_fusion = bf16[768,1536]{1,0:T(8,128)(2,1)} fusion(s32[264]{0:T(512)S(1)} %fusion.121, bf16[]{:T(256)} %constant.248.clone.1, bf16[33,1536]{1,0:T(8,128)(2,1)S(1)} %fusion.55), kind=kCustom, calls=%fused_computation.25 | custom fusion | bytes 2482178 | tf_op jit(solution)/shard_map/scatter | solution.py:422
  169.2 71.9 %all_to_all.10 = bf16[32,1,24,1536]{3,2,1,0:T(8,128)(2,1)S(1)} all-to-all(bf16[32,1,24,1536]{3,2,1,0:T(8,128)(2,1)} %bitcast.337), channel_id=1, replica_groups=mesh['seq'=32,'tp'=8] {'seq'}, dimensions={0} | all-to-all | bytes 4718592 | tf_op jit(solution)/shard_map/all_to_all | solution.py:426
  241.1 2.6 fusion.8
  243.7 3.0 fusion.6
  246.7 6.5 %all-to-all-start.1 = ((bf16[32,1,24,1536]{3,2,1,0:T(8,128)(2,1)}), bf16[32,1,24,1536]{3,2,1,0:T(8,128)(2,1)}, u32[]{:S(2)}, u32[]{:S(2)}) async-start(bf16[32,1,24,1536]{3,2,1,0:T(8,128)(2,1)} %fusion.6), calls=%async_computation.1 | async-start | bytes 4718592 | tf_op jit(solution)/shard_map/all_to_all | solution.py:435
  253.3 53.7 %all-to-all-done.1 = bf16[32,1,24,1536]{3,2,1,0:T(8,128)(2,1)} async-done(((bf16[32,1,24,1536]{3,2,1,0:T(8,128)(2,1)}), bf16[32,1,24,1536]{3,2,1,0:T(8,128)(2,1)}, u32[]{:S(2)}, u32[]{:S(2)}) %all-to-all-start.1) | async-done | bytes 2359328 | tf_op jit(solution)/shard_map/all_to_all | solution.py:435
  307.0 6.1 %gather_fusion = bf16[264,1536]{1,0:T(8,128)(2,1)} fusion(bf16[768,1536]{1,0:T(8,128)(2,1)} %bitcast.103, s32[1024]{0:T(1024)S(1)} %pad_clamp_fusion), kind=kCustom, calls=%fused_computation | custom fusion | bytes 1623072 | tf_op jit(solution)/shard_map/gather | solution.py:437
  313.1 2.0 fusion.13
  (214 shorter events, 55.9 us)
Async XLA Ops:
  7.2 233.9 %copy-start = (bf16[1,1536,1024]{2,1,0:T(8,128)(2,1)S(1)}, bf16[1,1536,1024]{2,1,0:T(8,128)(2,1)}, u32[]{:S(2)}) copy-start(bf16[1,1536,1024]{2,1,0:T(8,128)(2,1)} %param.24) | copy-start | bytes 9437188
  7.2 7.6 %copy-start.6 = (bf16[1,1536]{1,0:T(2,128)(2,1)S(1)}, bf16[1,1536]{1,0:T(2,128)(2,1)}, u32[]{:S(2)}) copy-start(bf16[1,1536]{1,0:T(2,128)(2,1)} %param.15) | copy-start | bytes 9220
  7.2 119.4 %all-gather.3.cloned.1.call-start = ((), (), s32[]{:S(2)}) async-start(), calls=%async_computation.2 | async-start | bytes 2162688 | tf_op jit(solution)/shard_map/all_gather | solution.py:279
  7.3 13.6 %copy-start.11 = (f32[32]{0:T(128)}, f32[32]{0:T(128)S(1)}, u32[]{:S(2)}) copy-start(f32[32]{0:T(128)S(1)} %multiply_power_fusion) | copy-start | bytes 388
  7.3 21.2 %copy-start.10 = (s32[256]{0:T(256)}, s32[256]{0:T(256)S(1)}, u32[]{:S(2)}) copy-start(s32[256]{0:T(256)S(1)} %get-tuple-element.69) | copy-start | bytes 3076
  14.8 8.1 %copy-start.14 = (s32[4]{0:T(128)S(1)}, s32[4]{0:T(128)}, u32[]{:S(2)}) copy-start(s32[4]{0:T(128)} %param.22) | copy-start | bytes 52
  14.8 8.8 %copy-start.9 = (s32[33,8]{0,1:T(8,128)S(1)}, s32[33,8]{0,1:T(8,128)}, u32[]{:S(2)}) copy-start(s32[33,8]{0,1:T(8,128)} %param.26) | copy-start | bytes 3172
  14.8 17.3 %collective-permute-start.3 = (bf16[1,12,128]{2,1,0:T(8,128)(2,1)S(1)}, bf16[1,12,128]{2,1,0:T(8,128)(2,1)}, u32[]{:S(2)}, u32[]{:S(2)}) collective-permute-start(bf16[1,12,128]{2,1,0:T(8,128)(2,1)S(1)} %bitcast.352), channel_id=1, source_target_pairs={{0,4},{1,5},{2,6},{3,7},{4,0},{5,1},{6,2},{7,3},{8,12},{9,13},{10,... | collective-permute-start | bytes 9224 | tf_op jit(solution)/shard_map/ppermute | solution.py:162
  23.0 1.4 copy-start.4
  23.8 0.6 copy-start.8
  32.2 4.5 %copy-start.15 = (f32[8]{0:T(128)}, f32[8]{0:T(128)S(1)}, u32[]{:S(2)}) copy-start(f32[8]{0:T(128)S(1)} %dynamic-slice_convert_fusion) | copy-start | bytes 100
  32.9 3.7 %collective-permute-start.4 = (bf16[2,1,12,128]{3,2,1,0:T(8,128)(2,1)S(1)}, bf16[2,1,12,128]{3,2,1,0:T(8,128)(2,1)S(1)}, u32[]{:S(2)}, u32[]{:S(2)}) collective-permute-start(bf16[2,1,12,128]{3,2,1,0:T(8,128)(2,1)S(1)} %pad_maximum_fusion.12), channel_id=1, source_target_pairs={{0,2},{1,3},{2,0},{3,1},{4,6},{5,7},{6,4},{7,5},{8,10},{9,11},{10,... | collective-permute-start | bytes 18440 | tf_op jit(solution)/shard_map/ppermute | solution.py:162
  36.7 1.3 collective-permute-start.5
  38.3 17.1 %copy-start.5 = (bf16[2,2,2,1,12,128]{5,4,2,1,0,3:T(8,128)(2,1)}, bf16[2,2,2,1,12,128]{5,4,2,1,0,3:T(8,128)(2,1)S(1)}, u32[]{:S(2)}) copy-start(bf16[2,2,2,1,12,128]{5,4,2,1,0,3:T(8,128)(2,1)S(1)} %copy.879) | copy-start | bytes 73732
  40.0 8.8 %collective-permute-start.6 = (bf16[1,12,128]{2,1,0:T(8,128)(2,1)S(1)}, bf16[1,12,128]{2,1,0:T(8,128)(2,1)S(1)}, u32[]{:S(2)}, u32[]{:S(2)}) collective-permute-start(bf16[1,12,128]{2,1,0:T(8,128)(2,1)S(1)} %convert_element_type.254), channel_id=1, source_target_pairs={{0,128},{8,136},{16,144},{24,152},{32,160},{40,168},{48,176},{56,1... | collective-permute-start | bytes 9224 | tf_op jit(solution)/shard_map/ppermute | solution.py:162
  48.8 4.6 %collective-permute-start.7 = (bf16[2,1,12,128]{3,2,0,1:T(8,128)(2,1)S(1)}, bf16[2,1,12,128]{3,2,0,1:T(8,128)(2,1)S(1)}, u32[]{:S(2)}, u32[]{:S(2)}) collective-permute-start(bf16[2,1,12,128]{3,2,0,1:T(8,128)(2,1)S(1)} %fusion.107), channel_id=1, source_target_pairs={{0,64},{8,72},{16,80},{24,88},{32,96},{40,104},{48,112},{56,120},{... | collective-permute-start | bytes 18440 | tf_op jit(solution)/shard_map/ppermute | solution.py:162
  53.5 3.8 %collective-permute-start.8 = (bf16[2,2,1,12,128]{4,3,0,1,2:T(8,128)(2,1)S(1)}, bf16[2,2,1,12,128]{4,3,0,1,2:T(8,128)(2,1)S(1)}, u32[]{:S(2)}, u32[]{:S(2)}) collective-permute-start(bf16[2,2,1,12,128]{4,3,0,1,2:T(8,128)(2,1)S(1)} %fusion.93), channel_id=1, source_target_pairs={{0,32},{8,40},{16,48},{24,56},{32,0},{40,8},{48,16},{56,24},{64,96... | collective-permute-start | bytes 36872 | tf_op jit(solution)/shard_map/ppermute | solution.py:162
  57.3 5.5 %collective-permute-start.9 = (bf16[2,2,2,1,12,128]{5,4,0,1,2,3:T(8,128)(2,1)S(1)}, bf16[2,2,2,1,12,128]{5,4,0,1,2,3:T(8,128)(2,1)S(1)}, u32[]{:S(2)}, u32[]{:S(2)}) collective-permute-start(bf16[2,2,2,1,12,128]{5,4,0,1,2,3:T(8,128)(2,1)S(1)} %fusion.89), channel_id=1, source_target_pairs={{0,16},{8,24},{16,0},{24,8},{32,48},{40,56},{48,32},{56,40},{64,80... | collective-permute-start | bytes 73736 | tf_op jit(solution)/shard_map/ppermute | solution.py:162
  62.9 6.5 %collective-permute-start.10 = (bf16[2,2,2,2,1,12,128]{6,5,0,1,2,3,4:T(8,128)(2,1)S(1)}, bf16[2,2,2,2,1,12,128]{6,5,0,1,2,3,4:T(8,128)(2,1)S(1)}, u32[]{:S(2)}, u32[]{:S(2)}) collective-permute-start(bf16[2,2,2,2,1,12,128]{6,5,0,1,2,3,4:T(8,128)(2,1)S(1)} %fusion.80), channel_id=1, source_target_pairs={{0,8},{8,0},{16,24},{24,16},{32,40},{40,32},{48,56},{56,48},{64,72... | collective-permute-start | bytes 147464 | tf_op jit(solution)/shard_map/ppermute | solution.py:162
  69.7 4.7 %copy-start.1 = (bf16[256,64,1,128]{3,1,2,0:T(8,128)(2,1)S(1)}, bf16[256,64,1,128]{3,1,2,0:T(8,128)(2,1)}, u32[]{:S(2)}) copy-start(bf16[256,64,1,128]{3,1,2,0:T(8,128)(2,1)} %param.20) | copy-start | bytes 12582916
  69.7 4.7 %copy-start.3 = (pred[256,64]{1,0:T(8,128)(4,1)S(1)}, pred[256,64]{1,0:T(8,128)(4,1)}, u32[]{:S(2)}) copy-start(pred[256,64]{1,0:T(8,128)(4,1)} %broadcast_compare_fusion) | copy-start | bytes 49156
  80.7 5.1 %collective-permute-start.11 = (f32[2,2,2,2,8,198]{5,4,3,2,1,0:T(8,128)S(1)}, f32[2,2,2,2,8,198]{5,4,3,2,1,0:T(8,128)S(1)}, u32[]{:S(2)}, u32[]{:S(2)}) collective-permute-start(f32[2,2,2,2,8,198]{5,4,3,2,1,0:T(8,128)S(1)} %get-tuple-element.28), channel_id=1, source_target_pairs={{0,8},{8,0},{16,24},{24,16},{32,40},{40,32},{48,56},{56,48},{64,72... | collective-permute-start | bytes 304136 | tf_op jit(solution)/shard_map/ppermute | solution.py:162
  85.8 0.8 copy-start.2
  91.6 5.9 %collective-permute-start.12 = (f32[2,2,2,8,198]{4,3,2,1,0:T(8,128)S(1)}, f32[2,2,2,8,198]{4,3,2,1,0:T(8,128)S(1)}, u32[]{:S(2)}, u32[]{:S(2)}) collective-permute-start(f32[2,2,2,8,198]{4,3,2,1,0:T(8,128)S(1)} %get-tuple-element.34), channel_id=1, source_target_pairs={{0,16},{8,24},{16,0},{24,8},{32,48},{40,56},{48,32},{56,40},{64,80... | collective-permute-start | bytes 152072 | tf_op jit(solution)/shard_map/ppermute | solution.py:162
  98.7 26.2 %copy-start.12 = (bf16[1536]{0:T(1024)(128)(2,1)S(1)}, bf16[1536]{0:T(1024)(128)(2,1)}, u32[]{:S(2)}) copy-start(bf16[1536]{0:T(1024)(128)(2,1)} %param.23) | copy-start | bytes 9220
  99.6 4.0 %collective-permute-start.13 = (f32[2,2,8,198]{3,2,1,0:T(8,128)S(1)}, f32[2,2,8,198]{3,2,1,0:T(8,128)S(1)}, u32[]{:S(2)}, u32[]{:S(2)}) collective-permute-start(f32[2,2,8,198]{3,2,1,0:T(8,128)S(1)} %get-tuple-element.36), channel_id=1, source_target_pairs={{0,32},{8,40},{16,48},{24,56},{32,0},{40,8},{48,16},{56,24},{64,96... | collective-permute-start | bytes 76040 | tf_op jit(solution)/shard_map/ppermute | solution.py:162
  104.2 4.7 %collective-permute-start.14 = (f32[2,8,198]{2,1,0:T(8,128)S(1)}, f32[2,8,198]{2,1,0:T(8,128)S(1)}, u32[]{:S(2)}, u32[]{:S(2)}) collective-permute-start(f32[2,8,198]{2,1,0:T(8,128)S(1)} %get-tuple-element.42), channel_id=1, source_target_pairs={{0,64},{8,72},{16,80},{24,88},{32,96},{40,104},{48,112},{56,120},{... | collective-permute-start | bytes 38024 | tf_op jit(solution)/shard_map/ppermute | solution.py:162
  109.5 7.6 %collective-permute-start.15 = (f32[8,198]{1,0:T(8,128)S(1)}, f32[8,198]{1,0:T(8,128)S(1)}, u32[]{:S(2)}, u32[]{:S(2)}) collective-permute-start(f32[8,198]{1,0:T(8,128)S(1)} %get-tuple-element.46), channel_id=1, source_target_pairs={{0,128},{8,136},{16,144},{24,152},{32,160},{40,168},{48,176},{56,1... | collective-permute-start | bytes 19016 | tf_op jit(solution)/shard_map/ppermute | solution.py:162
  119.7 5.2 %collective-permute-start.16 = (f32[2,2,12,128]{3,2,1,0:T(8,128)S(1)}, f32[2,2,12,128]{3,2,1,0:T(8,128)S(1)}, u32[]{:S(2)}, u32[]{:S(2)}) collective-permute-start(f32[2,2,12,128]{3,2,1,0:T(8,128)S(1)} %copy.914), channel_id=1, source_target_pairs={{0,1},{1,0},{2,3},{3,2},{4,5},{5,4},{6,7},{7,6},{8,9},{9,8},{10,11... | collective-permute-start | bytes 73736 | tf_op jit(solution)/shard_map/ppermute | solution.py:162
  125.0 21.3 %collective-permute-start.17 = (f32[2,12,128]{2,1,0:T(8,128)S(1)}, f32[2,12,128]{2,1,0:T(8,128)S(1)}, u32[]{:S(2)}, u32[]{:S(2)}) collective-permute-start(f32[2,12,128]{2,1,0:T(8,128)S(1)} %select_bitcast_fusion.8), channel_id=1, source_target_pairs={{0,2},{1,3},{2,0},{3,1},{4,6},{5,7},{6,4},{7,5},{8,10},{9,11},{10,... | collective-permute-start | bytes 36872 | tf_op jit(solution)/shard_map/ppermute | solution.py:162
  146.0 1.8 collective-permute-start
  146.3 12.2 %copy-start.7 = (bf16[1,1536]{1,0:T(2,128)(2,1)S(1)}, bf16[1,1536]{1,0:T(2,128)(2,1)}, u32[]{:S(2)}) copy-start(bf16[1,1536]{1,0:T(2,128)(2,1)} %param.15) | copy-start | bytes 9220
  146.3 5.2 %collective-permute-start.18 = (f32[12,128]{1,0:T(8,128)S(1)}, f32[12,128]{1,0:T(8,128)S(1)}, u32[]{:S(2)}, u32[]{:S(2)}) collective-permute-start(f32[12,128]{1,0:T(8,128)S(1)} %select_bitcast_fusion.12), channel_id=1, source_target_pairs={{0,4},{1,5},{2,6},{3,7},{4,0},{5,1},{6,2},{7,3},{8,12},{9,13},{10,... | collective-permute-start | bytes 18440 | tf_op jit(solution)/shard_map/ppermute | solution.py:162
  149.3 7.1 %collective-permute-start.1 = (bf16[2,384,128]{2,1,0:T(8,128)(2,1)S(1)}, bf16[2,384,128]{2,1,0:T(8,128)(2,1)S(1)}, u32[]{:S(2)}, u32[]{:S(2)}) collective-permute-start(bf16[2,384,128]{2,1,0:T(8,128)(2,1)S(1)} %fusion.60), channel_id=1, source_target_pairs={{0,2},{1,3},{2,0},{3,1},{4,6},{5,7},{6,4},{7,5},{8,10},{9,11},{10,... | collective-permute-start | bytes 589832 | tf_op jit(solution)/shard_map/ppermute | solution.py:162
  156.5 6.2 %collective-permute-start.2 = (bf16[384,128]{1,0:T(8,128)(2,1)S(1)}, bf16[384,128]{1,0:T(8,128)(2,1)S(1)}, u32[]{:S(2)}, u32[]{:S(2)}) collective-permute-start(bf16[384,128]{1,0:T(8,128)(2,1)S(1)} %fusion.72), channel_id=1, source_target_pairs={{0,4},{1,5},{2,6},{3,7},{4,0},{5,1},{6,2},{7,3},{8,12},{9,13},{10,... | collective-permute-start | bytes 294920 | tf_op jit(solution)/shard_map/ppermute | solution.py:162
  241.1 2.6 copy-start.16
  246.7 6.5 %copy-start.13 = (f32[33,8]{0,1:T(8,128)S(1)}, f32[33,8]{0,1:T(8,128)}, u32[]{:S(2)}) copy-start(f32[33,8]{0,1:T(8,128)} %param.27) | copy-start | bytes 3172
  246.7 60.3 %all-to-all-start.1 = ((bf16[32,1,24,1536]{3,2,1,0:T(8,128)(2,1)}), bf16[32,1,24,1536]{3,2,1,0:T(8,128)(2,1)}, u32[]{:S(2)}, u32[]{:S(2)}) async-start(bf16[32,1,24,1536]{3,2,1,0:T(8,128)(2,1)} %fusion.6), calls=%async_computation.1 | async-start | bytes 4718592 | tf_op jit(solution)/shard_map/all_to_all | solution.py:435
Sparse Core Ops, SparseCore 0:
  14.9 79.5 all-gather.2
where the time goes:
time: 325 us; the launch traced here: 323 us
  waiting for transfers between devices  81.9 us (25%)
  blocking collectives  71.9 us (22%)
  starting transfers between devices  42.4 us (13%)
  other arithmetic  42.1 us (13%)
  local copies, waits for them, and re-layouts  36.6 us (11%)
  matrix products  22.1 us (7%)
  between operations  14.8 us (5%)
  Pallas kernels  11.6 us (4%)
    all_to_all x1, blocking collectives, shards(): lax.all_to_all(outgoing, 'seq', split_axis=0, concat_axis=0, tiled=True)  71.9 us
    all_to_all x1, waiting for transfers between devices, shards(): lax.all_to_all(results, 'seq', split_axis=0, concat_axis=0, tiled=True)  53.7 us
    ppermute x19, starting transfers between devices, swap_partner(): return lax.ppermute(values, axis_name, pairs)  35.8 us
    ppermute x19, waiting for transfers between devices, swap_partner(): return lax.ppermute(values, axis_name, pairs)  28.1 us
    pallas_call x1, Pallas kernels, flash_attend(): pl.pallas_call(body, grid_spec=grid_spec, out_shape=jax.ShapeDtypeStruct(...  11.6 us
  transfers between devices with their start and end apart: 21, of which 16 were waited for; matrix products, arithmetic and copies ran while one was open for 22% of the time, Pallas kernels for 4%

commit v1 on v0

--- a/solution.py
+++ b/solution.py
@@ -85,7 +85,7 @@
 
 
 def flash_kernel(
-    flags_ref, q_ref, k_ref, v_ref, row_token_ref, row_tenant_ref, key_tenant_ref,
+    flags_ref, q_ref, kv_ref, row_token_ref, row_tenant_ref, key_tenant_ref,
     o_ref, max_ref, total_ref, acc_ref, *, score_scale, block_len
 ):
     step = pl.program_id(0)
@@ -100,7 +100,7 @@
     def _():
         scores = (
             lax.dot_general(
-                q_ref[...], v_ref[...], (((1,), (1,)), ((), ())),
+                q_ref[...], kv_ref[...], (((1,), (1,)), ((), ())),
                 preferred_element_type=jnp.float32,
             )
             * score_scale
@@ -116,7 +116,7 @@
         factor = jnp.exp(run_max - new_max)
         total_ref[...] = total_ref[...] * factor + jnp.sum(weights_exp, axis=-1, keepdims=True)
         acc_ref[...] = acc_ref[...] * factor + jnp.dot(
-            weights_exp.astype(jnp.bfloat16), v_ref[...], preferred_element_type=jnp.float32
+            weights_exp.astype(jnp.bfloat16), kv_ref[...], preferred_element_type=jnp.float32
         )
         max_ref[...] = new_max
 
@@ -134,7 +134,6 @@
         grid=(key_count // block_len,),
         in_specs=[
             pl.BlockSpec((query_count, head_dim), full),
-            pl.BlockSpec((block_len, head_dim), lambda step, flags_ref: (step, head)),
             pl.BlockSpec((block_len, head_dim), lambda step, flags_ref: (step, head)),
             pl.BlockSpec((query_count, 1), full),
             pl.BlockSpec((query_count, 1), full),
@@ -153,7 +152,7 @@
         grid_spec=grid_spec,
         out_shape=jax.ShapeDtypeStruct((query_count, head_dim), jnp.bfloat16),
         interpret=interpret,
-    )(flags, queries, keyvals, keyvals, row_token[:, None], row_tenant[:, None], key_tenant[None, :])
+    )(flags, queries, keyvals, row_token[:, None], row_tenant[:, None], key_tenant[None, :])
 
 
 def swap_partner(values, axis_name, distance):

time: 325 us -> 326 us (level)
  transfers between devices with their start and end apart: 21 -> 21, of which waited for: 16 -> 16; matrix products, arithmetic and copies ran while one was open for 22% -> 22% of each run, Pallas kernels for 4% -> 3%
where the time goes in v1:
time: 326 us; the launch traced here: 323 us
  waiting for transfers between devices  81.9 us (25%)
  blocking collectives  72.1 us (22%)
  starting transfers between devices  42.4 us (13%)
  other arithmetic  42.1 us (13%)
  local copies, waits for them, and re-layouts  36.6 us (11%)
  matrix products  22.1 us (7%)
  between operations  14.8 us (5%)
  Pallas kernels  10.9 us (3%)
    all_to_all x1, blocking collectives, shards(): lax.all_to_all(outgoing, 'seq', split_axis=0, concat_axis=0, tiled=True)  72.1 us
    all_to_all x1, waiting for transfers between devices, shards(): lax.all_to_all(results, 'seq', split_axis=0, concat_axis=0, tiled=True)  53.7 us
    ppermute x19, starting transfers between devices, swap_partner(): return lax.ppermute(values, axis_name, pairs)  35.8 us
    ppermute x19, waiting for transfers between devices, swap_partner(): return lax.ppermute(values, axis_name, pairs)  28.1 us
    pallas_call x1, Pallas kernels, flash_attend(): pl.pallas_call(body, grid_spec=grid_spec, out_shape=jax.ShapeDtypeStruct(...  10.9 us
  transfers between devices with their start and end apart: 21, of which 16 were waited for; matrix products, arithmetic and copies ran while one was open for 22% of the time, Pallas kernels for 3%

profile of v1, /device:TPU:10, one launch (start us, length us, event | category | flops | bytes accessed | tf_op | source)
XLA Modules:
  0.0 322.7 jit_solution(6580209966115522317)
XLA Ops:
  11.7 1.7 convolution_bitcast_fusion
  14.8 2.4 collective-permute-start.3
  19.0 1.8 fusion.58
  26.3 2.2 subtract_convert_fusion
  28.5 2.9 and_reduce_fusion
  32.9 1.4 collective-permute-start.4
  35.1 1.6 collective-permute-done.4
  40.0 7.2 %collective-permute-start.6 = (bf16[1,12,128]{2,1,0:T(8,128)(2,1)S(1)}, bf16[1,12,128]{2,1,0:T(8,128)(2,1)S(1)}, u32[]{:S(2)}, u32[]{:S(2)}) collective-permute-start(bf16[1,12,128]{2,1,0:T(8,128)(2,1)S(1)} %convert_element_type.254), channel_id=1, source_target_pairs={{0,128},{8,136},{16,144},{24,152},{32,160},{40,168},{48,176},{56,1... | collective-permute-start | bytes 9224 | tf_op jit(solution)/shard_map/ppermute | solution.py:161
  47.2 1.4 broadcast_compare_fusion
  48.8 2.1 collective-permute-start.7
  51.6 1.8 collective-permute-done.7
  55.4 1.9 collective-permute-done.8
  57.3 2.2 collective-permute-start.9
  60.2 1.8 concatenate.95
  62.9 1.6 collective-permute-start.10
  64.5 1.8 fusion.62.refs_1_
  66.4 2.3 dot_general.58
  69.7 4.7 %fusion.131 = (f32[256,3]{1,0:T(8,128)S(1)}, f32[256,3,64]{2,1,0:T(4,128)S(1)}) fusion(bf16[256,64,1,128]{3,1,2,0:T(8,128)(2,1)} %param.20, bf16[256,1,3,64]{3,2,0,1:T(4,128)(2,1)S(1)} %reshape.904, pred[256,64]{1,0:T(8,128)(4,1)} %broadcast_compare_fusion), kind=kOutput, calls=%fused_computation.296 | convolution fusion | flops 12729600 | bytes 4508672 | tf_op jit(solution)/shard_map/bhgd,bkhd->bhgk/dot_general | solution.py:348
  75.7 1.4 fusion.45
  78.2 1.4 concatenate.100
  81.4 1.8 fusion.132
  83.2 2.6 collective-permute-done.11
  91.6 1.6 collective-permute-start.12
  93.2 1.5 fusion.119
  94.6 2.8 collective-permute-done.12
  101.4 2.2 collective-permute-done.13
  104.2 2.1 collective-permute-start.14
  107.0 1.9 collective-permute-done.14
  109.5 6.0 %collective-permute-start.15 = (f32[8,198]{1,0:T(8,128)S(1)}, f32[8,198]{1,0:T(8,128)S(1)}, u32[]{:S(2)}, u32[]{:S(2)}) collective-permute-start(f32[8,198]{1,0:T(8,128)S(1)} %get-tuple-element.46), channel_id=1, source_target_pairs={{0,128},{8,136},{16,144},{24,152},{32,160},{40,168},{48,176},{56,1... | collective-permute-start | bytes 19016 | tf_op jit(solution)/shard_map/ppermute | solution.py:161
  115.7 1.4 collective-permute-done.15
  125.0 1.6 collective-permute-start.17
  126.6 10.9 %shard_map.149 = bf16[768,128]{1,0:T(8,128)(2,1)} custom-call(s32[16]{0:T(128)} %convert_element_type.234.refs_0_, bf16[768,128]{1,0:T(8,128)(2,1)} %fusion.62.refs_1_, bf16[8192,128]{1,0:T(8,128)(2,1)} %bitcast.340, s32[768,1]{1,0:T(8,128)} %broadcast_in_dim_reshape.9.refs_3_, s32[768,1]{1,0:T(8,128)} %broadcast_in_dim_reshape.10.refs_4_, s32[1,8192]{1,0:T(1,128)} %bitcast.344), custom_call_target="tpu_custom_call" | custom-call | tf_op jit(solution)/shard_map/pallas_call | solution.py:150
  138.7 2.6 fusion.133
  141.3 2.5 reshape.902
  143.8 1.4 fusion.38
  147.0 1.5 fusion.32
  148.5 1.5 collective-permute-start.1
  150.8 4.9 %collective-permute-done.1 = bf16[2,384,128]{2,1,0:T(8,128)(2,1)S(1)} collective-permute-done((bf16[2,384,128]{2,1,0:T(8,128)(2,1)S(1)}, bf16[2,384,128]{2,1,0:T(8,128)(2,1)S(1)}, u32[]{:S(2)}, u32[]{:S(2)}) %collective-permute-start.1) | collective-permute-done | bytes 196640 | tf_op jit(solution)/shard_map/ppermute | solution.py:161
  155.7 2.0 collective-permute-start.2
  157.8 4.2 %collective-permute-done.2 = bf16[384,128]{1,0:T(8,128)(2,1)S(1)} collective-permute-done((bf16[384,128]{1,0:T(8,128)(2,1)S(1)}, bf16[384,128]{1,0:T(8,128)(2,1)S(1)}, u32[]{:S(2)}, u32[]{:S(2)}) %collective-permute-start.2) | collective-permute-done | bytes 98336 | tf_op jit(solution)/shard_map/ppermute | solution.py:161
  164.8 3.6 %scatter_custom_fusion = bf16[768,1536]{1,0:T(8,128)(2,1)} fusion(s32[264]{0:T(512)S(1)} %fusion.121, bf16[]{:T(256)} %constant.248.clone.1, bf16[33,1536]{1,0:T(8,128)(2,1)S(1)} %fusion.55), kind=kCustom, calls=%fused_computation.25 | custom fusion | bytes 2482178 | tf_op jit(solution)/shard_map/scatter | solution.py:421
  168.4 72.1 %all_to_all.10 = bf16[32,1,24,1536]{3,2,1,0:T(8,128)(2,1)S(1)} all-to-all(bf16[32,1,24,1536]{3,2,1,0:T(8,128)(2,1)} %bitcast.337), channel_id=1, replica_groups=mesh['seq'=32,'tp'=8] {'seq'}, dimensions={0} | all-to-all | bytes 4718592 | tf_op jit(solution)/shard_map/all_to_all | solution.py:425
  240.5 2.6 fusion.8
  243.2 3.0 fusion.6
  246.1 6.5 %all-to-all-start.1 = ((bf16[32,1,24,1536]{3,2,1,0:T(8,128)(2,1)}), bf16[32,1,24,1536]{3,2,1,0:T(8,128)(2,1)}, u32[]{:S(2)}, u32[]{:S(2)}) async-start(bf16[32,1,24,1536]{3,2,1,0:T(8,128)(2,1)} %fusion.6), calls=%async_computation.1 | async-start | bytes 4718592 | tf_op jit(solution)/shard_map/all_to_all | solution.py:434
  252.7 53.7 %all-to-all-done.1 = bf16[32,1,24,1536]{3,2,1,0:T(8,128)(2,1)} async-done(((bf16[32,1,24,1536]{3,2,1,0:T(8,128)(2,1)}), bf16[32,1,24,1536]{3,2,1,0:T(8,128)(2,1)}, u32[]{:S(2)}, u32[]{:S(2)}) %all-to-all-start.1) | async-done | bytes 2359328 | tf_op jit(solution)/shard_map/all_to_all | solution.py:434
  306.5 6.1 %gather_fusion = bf16[264,1536]{1,0:T(8,128)(2,1)} fusion(bf16[768,1536]{1,0:T(8,128)(2,1)} %bitcast.103, s32[1024]{0:T(1024)S(1)} %pad_clamp_fusion), kind=kCustom, calls=%fused_computation | custom fusion | bytes 1623072 | tf_op jit(solution)/shard_map/gather | solution.py:436
  312.5 2.0 fusion.13
  (214 shorter events, 55.9 us)
Async XLA Ops:
  7.2 233.4 %copy-start = (bf16[1,1536,1024]{2,1,0:T(8,128)(2,1)S(1)}, bf16[1,1536,1024]{2,1,0:T(8,128)(2,1)}, u32[]{:S(2)}) copy-start(bf16[1,1536,1024]{2,1,0:T(8,128)(2,1)} %param.24) | copy-start | bytes 9437188
  7.2 7.6 %copy-start.6 = (bf16[1,1536]{1,0:T(2,128)(2,1)S(1)}, bf16[1,1536]{1,0:T(2,128)(2,1)}, u32[]{:S(2)}) copy-start(bf16[1,1536]{1,0:T(2,128)(2,1)} %param.15) | copy-start | bytes 9220
  7.2 119.4 %all-gather.3.cloned.1.call-start = ((), (), s32[]{:S(2)}) async-start(), calls=%async_computation.2 | async-start | bytes 2162688 | tf_op jit(solution)/shard_map/all_gather | solution.py:278
  7.3 13.6 %copy-start.11 = (f32[32]{0:T(128)}, f32[32]{0:T(128)S(1)}, u32[]{:S(2)}) copy-start(f32[32]{0:T(128)S(1)} %multiply_power_fusion) | copy-start | bytes 388
  7.3 21.2 %copy-start.10 = (s32[256]{0:T(256)}, s32[256]{0:T(256)S(1)}, u32[]{:S(2)}) copy-start(s32[256]{0:T(256)S(1)} %get-tuple-element.69) | copy-start | bytes 3076
  14.8 8.1 %copy-start.14 = (s32[4]{0:T(128)S(1)}, s32[4]{0:T(128)}, u32[]{:S(2)}) copy-start(s32[4]{0:T(128)} %param.22) | copy-start | bytes 52
  14.8 8.8 %copy-start.9 = (s32[33,8]{0,1:T(8,128)S(1)}, s32[33,8]{0,1:T(8,128)}, u32[]{:S(2)}) copy-start(s32[33,8]{0,1:T(8,128)} %param.26) | copy-start | bytes 3172
  14.8 17.3 %collective-permute-start.3 = (bf16[1,12,128]{2,1,0:T(8,128)(2,1)S(1)}, bf16[1,12,128]{2,1,0:T(8,128)(2,1)}, u32[]{:S(2)}, u32[]{:S(2)}) collective-permute-start(bf16[1,12,128]{2,1,0:T(8,128)(2,1)S(1)} %bitcast.351), channel_id=1, source_target_pairs={{0,4},{1,5},{2,6},{3,7},{4,0},{5,1},{6,2},{7,3},{8,12},{9,13},{10,... | collective-permute-start | bytes 9224 | tf_op jit(solution)/shard_map/ppermute | solution.py:161
  23.0 1.4 copy-start.4
  23.8 0.6 copy-start.8
  32.2 4.5 %copy-start.15 = (f32[8]{0:T(128)}, f32[8]{0:T(128)S(1)}, u32[]{:S(2)}) copy-start(f32[8]{0:T(128)S(1)} %dynamic-slice_convert_fusion) | copy-start | bytes 100
  32.9 3.7 %collective-permute-start.4 = (bf16[2,1,12,128]{3,2,1,0:T(8,128)(2,1)S(1)}, bf16[2,1,12,128]{3,2,1,0:T(8,128)(2,1)S(1)}, u32[]{:S(2)}, u32[]{:S(2)}) collective-permute-start(bf16[2,1,12,128]{3,2,1,0:T(8,128)(2,1)S(1)} %pad_maximum_fusion.12), channel_id=1, source_target_pairs={{0,2},{1,3},{2,0},{3,1},{4,6},{5,7},{6,4},{7,5},{8,10},{9,11},{10,... | collective-permute-start | bytes 18440 | tf_op jit(solution)/shard_map/ppermute | solution.py:161
  36.7 1.3 collective-permute-start.5
  38.3 17.1 %copy-start.5 = (bf16[2,2,2,1,12,128]{5,4,2,1,0,3:T(8,128)(2,1)}, bf16[2,2,2,1,12,128]{5,4,2,1,0,3:T(8,128)(2,1)S(1)}, u32[]{:S(2)}) copy-start(bf16[2,2,2,1,12,128]{5,4,2,1,0,3:T(8,128)(2,1)S(1)} %copy.879) | copy-start | bytes 73732
  40.0 8.8 %collective-permute-start.6 = (bf16[1,12,128]{2,1,0:T(8,128)(2,1)S(1)}, bf16[1,12,128]{2,1,0:T(8,128)(2,1)S(1)}, u32[]{:S(2)}, u32[]{:S(2)}) collective-permute-start(bf16[1,12,128]{2,1,0:T(8,128)(2,1)S(1)} %convert_element_type.254), channel_id=1, source_target_pairs={{0,128},{8,136},{16,144},{24,152},{32,160},{40,168},{48,176},{56,1... | collective-permute-start | bytes 9224 | tf_op jit(solution)/shard_map/ppermute | solution.py:161
  48.8 4.6 %collective-permute-start.7 = (bf16[2,1,12,128]{3,2,0,1:T(8,128)(2,1)S(1)}, bf16[2,1,12,128]{3,2,0,1:T(8,128)(2,1)S(1)}, u32[]{:S(2)}, u32[]{:S(2)}) collective-permute-start(bf16[2,1,12,128]{3,2,0,1:T(8,128)(2,1)S(1)} %fusion.107), channel_id=1, source_target_pairs={{0,64},{8,72},{16,80},{24,88},{32,96},{40,104},{48,112},{56,120},{... | collective-permute-start | bytes 18440 | tf_op jit(solution)/shard_map/ppermute | solution.py:161
  53.5 3.8 %collective-permute-start.8 = (bf16[2,2,1,12,128]{4,3,0,1,2:T(8,128)(2,1)S(1)}, bf16[2,2,1,12,128]{4,3,0,1,2:T(8,128)(2,1)S(1)}, u32[]{:S(2)}, u32[]{:S(2)}) collective-permute-start(bf16[2,2,1,12,128]{4,3,0,1,2:T(8,128)(2,1)S(1)} %fusion.93), channel_id=1, source_target_pairs={{0,32},{8,40},{16,48},{24,56},{32,0},{40,8},{48,16},{56,24},{64,96... | collective-permute-start | bytes 36872 | tf_op jit(solution)/shard_map/ppermute | solution.py:161
  57.3 5.5 %collective-permute-start.9 = (bf16[2,2,2,1,12,128]{5,4,0,1,2,3:T(8,128)(2,1)S(1)}, bf16[2,2,2,1,12,128]{5,4,0,1,2,3:T(8,128)(2,1)S(1)}, u32[]{:S(2)}, u32[]{:S(2)}) collective-permute-start(bf16[2,2,2,1,12,128]{5,4,0,1,2,3:T(8,128)(2,1)S(1)} %fusion.89), channel_id=1, source_target_pairs={{0,16},{8,24},{16,0},{24,8},{32,48},{40,56},{48,32},{56,40},{64,80... | collective-permute-start | bytes 73736 | tf_op jit(solution)/shard_map/ppermute | solution.py:161
  62.9 6.5 %collective-permute-start.10 = (bf16[2,2,2,2,1,12,128]{6,5,0,1,2,3,4:T(8,128)(2,1)S(1)}, bf16[2,2,2,2,1,12,128]{6,5,0,1,2,3,4:T(8,128)(2,1)S(1)}, u32[]{:S(2)}, u32[]{:S(2)}) collective-permute-start(bf16[2,2,2,2,1,12,128]{6,5,0,1,2,3,4:T(8,128)(2,1)S(1)} %fusion.80), channel_id=1, source_target_pairs={{0,8},{8,0},{16,24},{24,16},{32,40},{40,32},{48,56},{56,48},{64,72... | collective-permute-start | bytes 147464 | tf_op jit(solution)/shard_map/ppermute | solution.py:161
  69.7 4.7 %copy-start.1 = (bf16[256,64,1,128]{3,1,2,0:T(8,128)(2,1)S(1)}, bf16[256,64,1,128]{3,1,2,0:T(8,128)(2,1)}, u32[]{:S(2)}) copy-start(bf16[256,64,1,128]{3,1,2,0:T(8,128)(2,1)} %param.20) | copy-start | bytes 12582916
  69.7 4.7 %copy-start.3 = (pred[256,64]{1,0:T(8,128)(4,1)S(1)}, pred[256,64]{1,0:T(8,128)(4,1)}, u32[]{:S(2)}) copy-start(pred[256,64]{1,0:T(8,128)(4,1)} %broadcast_compare_fusion) | copy-start | bytes 49156
  80.7 5.1 %collective-permute-start.11 = (f32[2,2,2,2,8,198]{5,4,3,2,1,0:T(8,128)S(1)}, f32[2,2,2,2,8,198]{5,4,3,2,1,0:T(8,128)S(1)}, u32[]{:S(2)}, u32[]{:S(2)}) collective-permute-start(f32[2,2,2,2,8,198]{5,4,3,2,1,0:T(8,128)S(1)} %get-tuple-element.28), channel_id=1, source_target_pairs={{0,8},{8,0},{16,24},{24,16},{32,40},{40,32},{48,56},{56,48},{64,72... | collective-permute-start | bytes 304136 | tf_op jit(solution)/shard_map/ppermute | solution.py:161
  85.8 0.8 copy-start.2
  91.6 5.9 %collective-permute-start.12 = (f32[2,2,2,8,198]{4,3,2,1,0:T(8,128)S(1)}, f32[2,2,2,8,198]{4,3,2,1,0:T(8,128)S(1)}, u32[]{:S(2)}, u32[]{:S(2)}) collective-permute-start(f32[2,2,2,8,198]{4,3,2,1,0:T(8,128)S(1)} %get-tuple-element.34), channel_id=1, source_target_pairs={{0,16},{8,24},{16,0},{24,8},{32,48},{40,56},{48,32},{56,40},{64,80... | collective-permute-start | bytes 152072 | tf_op jit(solution)/shard_map/ppermute | solution.py:161
  98.7 26.2 %copy-start.12 = (bf16[1536]{0:T(1024)(128)(2,1)S(1)}, bf16[1536]{0:T(1024)(128)(2,1)}, u32[]{:S(2)}) copy-start(bf16[1536]{0:T(1024)(128)(2,1)} %param.23) | copy-start | bytes 9220
  99.6 4.0 %collective-permute-start.13 = (f32[2,2,8,198]{3,2,1,0:T(8,128)S(1)}, f32[2,2,8,198]{3,2,1,0:T(8,128)S(1)}, u32[]{:S(2)}, u32[]{:S(2)}) collective-permute-start(f32[2,2,8,198]{3,2,1,0:T(8,128)S(1)} %get-tuple-element.36), channel_id=1, source_target_pairs={{0,32},{8,40},{16,48},{24,56},{32,0},{40,8},{48,16},{56,24},{64,96... | collective-permute-start | bytes 76040 | tf_op jit(solution)/shard_map/ppermute | solution.py:161
  104.2 4.7 %collective-permute-start.14 = (f32[2,8,198]{2,1,0:T(8,128)S(1)}, f32[2,8,198]{2,1,0:T(8,128)S(1)}, u32[]{:S(2)}, u32[]{:S(2)}) collective-permute-start(f32[2,8,198]{2,1,0:T(8,128)S(1)} %get-tuple-element.42), channel_id=1, source_target_pairs={{0,64},{8,72},{16,80},{24,88},{32,96},{40,104},{48,112},{56,120},{... | collective-permute-start | bytes 38024 | tf_op jit(solution)/shard_map/ppermute | solution.py:161
  109.5 7.6 %collective-permute-start.15 = (f32[8,198]{1,0:T(8,128)S(1)}, f32[8,198]{1,0:T(8,128)S(1)}, u32[]{:S(2)}, u32[]{:S(2)}) collective-permute-start(f32[8,198]{1,0:T(8,128)S(1)} %get-tuple-element.46), channel_id=1, source_target_pairs={{0,128},{8,136},{16,144},{24,152},{32,160},{40,168},{48,176},{56,1... | collective-permute-start | bytes 19016 | tf_op jit(solution)/shard_map/ppermute | solution.py:161
  119.7 5.2 %collective-permute-start.16 = (f32[2,2,12,128]{3,2,1,0:T(8,128)S(1)}, f32[2,2,12,128]{3,2,1,0:T(8,128)S(1)}, u32[]{:S(2)}, u32[]{:S(2)}) collective-permute-start(f32[2,2,12,128]{3,2,1,0:T(8,128)S(1)} %copy.914), channel_id=1, source_target_pairs={{0,1},{1,0},{2,3},{3,2},{4,5},{5,4},{6,7},{7,6},{8,9},{9,8},{10,11... | collective-permute-start | bytes 73736 | tf_op jit(solution)/shard_map/ppermute | solution.py:161
  125.0 20.5 %collective-permute-start.17 = (f32[2,12,128]{2,1,0:T(8,128)S(1)}, f32[2,12,128]{2,1,0:T(8,128)S(1)}, u32[]{:S(2)}, u32[]{:S(2)}) collective-permute-start(f32[2,12,128]{2,1,0:T(8,128)S(1)} %select_bitcast_fusion.8), channel_id=1, source_target_pairs={{0,2},{1,3},{2,0},{3,1},{4,6},{5,7},{6,4},{7,5},{8,10},{9,11},{10,... | collective-permute-start | bytes 36872 | tf_op jit(solution)/shard_map/ppermute | solution.py:161
  145.2 1.8 collective-permute-start
  145.5 12.2 %copy-start.7 = (bf16[1,1536]{1,0:T(2,128)(2,1)S(1)}, bf16[1,1536]{1,0:T(2,128)(2,1)}, u32[]{:S(2)}) copy-start(bf16[1,1536]{1,0:T(2,128)(2,1)} %param.15) | copy-start | bytes 9220
  145.5 5.2 %collective-permute-start.18 = (f32[12,128]{1,0:T(8,128)S(1)}, f32[12,128]{1,0:T(8,128)S(1)}, u32[]{:S(2)}, u32[]{:S(2)}) collective-permute-start(f32[12,128]{1,0:T(8,128)S(1)} %select_bitcast_fusion.12), channel_id=1, source_target_pairs={{0,4},{1,5},{2,6},{3,7},{4,0},{5,1},{6,2},{7,3},{8,12},{9,13},{10,... | collective-permute-start | bytes 18440 | tf_op jit(solution)/shard_map/ppermute | solution.py:161
  148.5 7.1 %collective-permute-start.1 = (bf16[2,384,128]{2,1,0:T(8,128)(2,1)S(1)}, bf16[2,384,128]{2,1,0:T(8,128)(2,1)S(1)}, u32[]{:S(2)}, u32[]{:S(2)}) collective-permute-start(bf16[2,384,128]{2,1,0:T(8,128)(2,1)S(1)} %fusion.60), channel_id=1, source_target_pairs={{0,2},{1,3},{2,0},{3,1},{4,6},{5,7},{6,4},{7,5},{8,10},{9,11},{10,... | collective-permute-start | bytes 589832 | tf_op jit(solution)/shard_map/ppermute | solution.py:161
  155.7 6.2 %collective-permute-start.2 = (bf16[384,128]{1,0:T(8,128)(2,1)S(1)}, bf16[384,128]{1,0:T(8,128)(2,1)S(1)}, u32[]{:S(2)}, u32[]{:S(2)}) collective-permute-start(bf16[384,128]{1,0:T(8,128)(2,1)S(1)} %fusion.72), channel_id=1, source_target_pairs={{0,4},{1,5},{2,6},{3,7},{4,0},{5,1},{6,2},{7,3},{8,12},{9,13},{10,... | collective-permute-start | bytes 294920 | tf_op jit(solution)/shard_map/ppermute | solution.py:161
  240.5 2.6 copy-start.16
  246.1 6.5 %copy-start.13 = (f32[33,8]{0,1:T(8,128)S(1)}, f32[33,8]{0,1:T(8,128)}, u32[]{:S(2)}) copy-start(f32[33,8]{0,1:T(8,128)} %param.27) | copy-start | bytes 3172
  246.1 60.3 %all-to-all-start.1 = ((bf16[32,1,24,1536]{3,2,1,0:T(8,128)(2,1)}), bf16[32,1,24,1536]{3,2,1,0:T(8,128)(2,1)}, u32[]{:S(2)}, u32[]{:S(2)}) async-start(bf16[32,1,24,1536]{3,2,1,0:T(8,128)(2,1)} %fusion.6), calls=%async_computation.1 | async-start | bytes 4718592 | tf_op jit(solution)/shard_map/all_to_all | solution.py:434
Sparse Core Ops, SparseCore 0:
  14.9 79.5 all-gather.2
